TPU v7x, 32 devices: a whole 2x2x4 slice. The times are simulated.
32 devices in a mesh: row: 8 (over y, x, core), col: 4 (over z).
Axes of the slice: x: 2, y: 2, z: 4, core: 2. Of those that a mesh axis runs over, the one named last changes fastest.
Arguments:
- tokens: bfloat16 [512, 8192], P('col', 'row'), may hold values from -6 to 6
- cotangent: bfloat16 [512, 8192], P('col', 'row'), may hold values from -1.5 to 1.5
- gate_weight: bfloat16 [8192, 28672], P('row', 'col'), may hold values from -0.0625 to 0.0625
- up_weight: bfloat16 [8192, 28672], P('row', 'col'), may hold values from -0.0625 to 0.0625
- down_weight: bfloat16 [28672, 8192], P('col', 'row'), may hold values from -0.03125 to 0.03125
Outputs:
- input_grad: bfloat16 [512, 8192], P('col', 'row')
- gate_grad: bfloat16 [8192, 28672], P('row', 'col')
- up_grad: bfloat16 [8192, 28672], P('row', 'col')
- down_grad: bfloat16 [28672, 8192], P('col', 'row')
All inputs are finite; a program needn't handle non-finite values.
Results may differ from a plain program's by a relative error of at most 0.02.
Values may be sent and summed in bfloat16 or wider, within the bound.
No kernel may reach another device: no remote copies, remote signals or barrier semaphores. Data moves between devices by JAX's collectives and lax.ppermute only.
A program may use at most 256 MiB of HBM per device.

v0:
```python
import jax
import jax.numpy as jnp
from jax import lax
from jax.sharding import PartitionSpec as P


def activations(sums, columns):
    gate = sums[:, :columns]
    up = sums[:, columns : 2 * columns]
    back = sums[:, 2 * columns :]
    sigma = jax.nn.sigmoid(gate)
    silu_gate = gate * sigma
    hidden = (silu_gate * up).astype(jnp.bfloat16)
    grad_gate_act = (back * up * sigma * (1.0 + gate * (1.0 - sigma))).astype(jnp.bfloat16)
    grad_up_act = (back * silu_gate).astype(jnp.bfloat16)
    return jnp.concatenate([hidden, grad_gate_act, grad_up_act], axis=1)


def contract_rows(left, right):
    return lax.dot_general(
        left, right, (((0,), (0,)), ((), ())), preferred_element_type=jnp.float32
    )


def contract_cols(left, right):
    return lax.dot_general(
        left, right, (((1,), (1,)), ((), ())), preferred_element_type=jnp.float32
    )


def per_device(tokens, cotangent, gate_weight, up_weight, down_weight):
    x_panel, dy_panel = (
        lax.all_gather(tokens, "col", axis=0, tiled=True),
        lax.all_gather(cotangent, "col", axis=0, tiled=True),
    )
    columns = gate_weight.shape[1]
    gate_part = jnp.dot(x_panel, gate_weight, preferred_element_type=jnp.float32)
    up_part = jnp.dot(x_panel, up_weight, preferred_element_type=jnp.float32)
    back_part = contract_cols(dy_panel, down_weight)
    sums = lax.psum_scatter(
        jnp.concatenate([gate_part, up_part, back_part], axis=1).astype(jnp.bfloat16),
        "row",
        scatter_dimension=0,
        tiled=True,
    ).astype(jnp.float32)
    packed = lax.all_gather(activations(sums, columns), "row", axis=0, tiled=True)
    hidden = packed[:, :columns]
    grad_gate_act = packed[:, columns : 2 * columns]
    grad_up_act = packed[:, 2 * columns :]
    down_grad = contract_rows(hidden, dy_panel).astype(jnp.bfloat16)
    gate_grad = contract_rows(x_panel, grad_gate_act).astype(jnp.bfloat16)
    up_grad = contract_rows(x_panel, grad_up_act).astype(jnp.bfloat16)
    input_sum = lax.psum_scatter(
        (contract_cols(grad_gate_act, gate_weight) + contract_cols(grad_up_act, up_weight)).astype(
            jnp.bfloat16
        ),
        "col",
        scatter_dimension=0,
        tiled=True,
    )
    return (input_sum, gate_grad, up_grad, down_grad)


def solution(mesh):
    in_specs = (P("col", "row"), P("col", "row"), P("row", "col"), P("row", "col"), P("col", "row"))
    out_specs = (P("col", "row"), P("row", "col"), P("row", "col"), P("col", "row"))
    return jax.shard_map(
        per_device, mesh=mesh, in_specs=in_specs, out_specs=out_specs, check_vma=False
    )
```

profile of v0, /device:TPU:0, one launch (start us, length us, event | category | flops | bytes accessed | tf_op | source)
XLA Modules:
  0.0 476.8 jit_solution(14434081499963626001)
XLA Ops:
  7.2 0.0 all-gather.4.cloned.1.call-start
  7.2 0.7 all-gather.4.cloned.1.call-update
  7.9 0.0 all-gather.6.cloned.1.call-start
  7.9 0.7 all-gather.6.cloned.1.call-update
  8.6 0.0 reduce-scatter.3.cloned.1.call-start
  8.7 31.5 %all-gather.4.cloned.1.call-done = bf16[512,1024]{1,0:T(8,128)(2,1)} async-done(((bf16[128,1024]{1,0:T(8,128)(2,1)}), bf16[512,1024]{1,0:T(8,128)(2,1)}) %all-gather.4.cloned.1.call-update) | async-done | bytes 1048592 | tf_op jit(solution)/shard_map/all_gather | solution.py:33
  40.2 0.0 copy-start
  40.2 15.1 %convolution_convert_fusion.2 = bf16[512,7168]{1,0:T(8,128)(2,1)} fusion(bf16[512,1024]{1,0:T(8,128)(2,1)} %all-gather.4.cloned.1.call-done, bf16[1024,7168]{1,0:T(8,128)(2,1)} %param.8), kind=kOutput, calls=%fused_computation.5 | convolution fusion | flops 7519862784 | bytes 23068672 | tf_op jit(solution)/shard_map/dot_general | solution.py:38
  55.3 0.0 copy-done
  55.3 15.0 %convolution_convert_fusion.3 = bf16[512,7168]{1,0:T(8,128)(2,1)} fusion(bf16[512,1024]{1,0:T(8,128)(2,1)S(1)} %copy-done, bf16[1024,7168]{1,0:T(8,128)(2,1)} %param.7), kind=kOutput, calls=%fused_computation.6 | convolution fusion | flops 7519862784 | bytes 23068672 | tf_op jit(solution)/shard_map/dot_general | solution.py:37
  70.3 0.0 all-gather.6.cloned.1.call-done
  70.4 13.2 %convolution_convert_fusion.1 = bf16[512,7168]{1,0:T(8,128)(2,1)} fusion(bf16[512,1024]{1,0:T(8,128)(2,1)} %all-gather.6.cloned.1.call-done, bf16[7168,1024]{1,0:T(8,128)(2,1)} %param.9), kind=kOutput, calls=%fused_computation.4 | convolution fusion | flops 7519862784 | bytes 23068672 | tf_op jit(solution)/shard_map/dot_general | solution.py:26
  83.5 19.6 %pad_maximum_fusion = bf16[512,21504]{1,0:T(8,128)(2,1)} fusion(bf16[512,7168]{1,0:T(8,128)(2,1)} %convolution_convert_fusion.1, bf16[512,7168]{1,0:T(8,128)(2,1)} %convolution_convert_fusion.2, bf16[512,7168]{1,0:T(8,128)(2,1)} %convolution_convert_fusion.3), kind=kLoop, calls=%fused_computation | loop fusion | flops 66060288 | bytes 44040192 | tf_op jit(solution)/shard_map/concatenate | solution.py:41
  103.1 0.0 reduce-scatter.3.cloned.1.call-update
  103.1 0.0 all-gather.8.cloned.1.call-start
  103.2 140.3 %reduce-scatter.3.cloned.1.call-done = bf16[64,21504]{1,0:T(8,128)(2,1)} async-done(((bf16[512,21504]{1,0:T(8,128)(2,1)}), bf16[64,21504]{1,0:T(8,128)(2,1)}) %reduce-scatter.3.cloned.1.call-update) | async-done | bytes 2752528 | tf_op jit(solution)/shard_map/reduce_scatter | solution.py:40
  243.5 2.1 convert_element_type.31
  245.6 1.1 multiply_convert_fusion.2
  246.7 1.7 pad_maximum_fusion.1
  248.4 0.0 all-gather.8.cloned.1.call-update
  248.4 0.2 reduce-scatter.5.cloned.1.call-start
  248.6 112.0 %all-gather.8.cloned.1.call-done = bf16[512,21504]{1,0:T(8,128)(2,1)} async-done(((bf16[64,21504]{1,0:T(8,128)(2,1)}), bf16[512,21504]{1,0:T(8,128)(2,1)}) %all-gather.8.cloned.1.call-update) | async-done | bytes 22020112 | tf_op jit(solution)/shard_map/all_gather | solution.py:46
  360.6 13.2 %fusion.2 = f32[512,1024]{1,0:T(8,128)S(1)} fusion(bf16[1024,7168]{1,0:T(8,128)(2,1)} %param.8, bf16[512,21504]{1,0:T(8,128)(2,1)} %all-gather.8.cloned.1.call-done), kind=kOutput, calls=%fused_computation.9 | convolution fusion | flops 7516192768 | bytes 24117248 | tf_op jit(solution)/shard_map/dot_general | solution.py:26
  373.7 14.0 %add_convert_fusion = bf16[512,1024]{1,0:T(8,128)(2,1)} fusion(f32[512,1024]{1,0:T(8,128)S(1)} %fusion.2, bf16[1024,7168]{1,0:T(8,128)(2,1)} %param.7, bf16[512,21504]{1,0:T(8,128)(2,1)} %all-gather.8.cloned.1.call-done), kind=kOutput, calls=%fused_computation.15 | convolution fusion | flops 7517241344 | bytes 25165824 | tf_op jit(solution)/shard_map/dot_general | solution.py:26
  387.8 0.0 reduce-scatter.5.cloned.1.call-update
  387.8 14.2 %convert_bitcast_fusion = bf16[1024,7168]{0,1:T(8,128)(2,1)} fusion(bf16[512,1024]{1,0:T(8,128)(2,1)S(1)} %copy-done, bf16[512,21504]{1,0:T(8,128)(2,1)} %all-gather.8.cloned.1.call-done), kind=kOutput, calls=%fused_computation.1 | convolution fusion | flops 7523532800 | bytes 23068672 | tf_op jit(solution)/shard_map/dot_general | solution.py:20
  402.0 19.9 %copy.10 = bf16[1024,7168]{1,0:T(8,128)(2,1)} copy(bf16[1024,7168]{0,1:T(8,128)(2,1)} %convert_bitcast_fusion) | data formatting | bytes 29360128
  421.9 14.2 %convert_bitcast_fusion.1 = bf16[1024,7168]{0,1:T(8,128)(2,1)} fusion(bf16[512,1024]{1,0:T(8,128)(2,1)S(1)} %copy-done, bf16[512,21504]{1,0:T(8,128)(2,1)} %all-gather.8.cloned.1.call-done), kind=kOutput, calls=%fused_computation.2 | convolution fusion | flops 7523532800 | bytes 23068672 | tf_op jit(solution)/shard_map/dot_general | solution.py:20
  436.1 0.0 copy-start.1
  436.1 20.0 %copy.9 = bf16[1024,7168]{1,0:T(8,128)(2,1)} copy(bf16[1024,7168]{0,1:T(8,128)(2,1)} %convert_bitcast_fusion.1) | data formatting | bytes 29360128
  456.1 0.0 copy-done.1
  456.1 14.2 %convolution_convert_fusion = bf16[7168,1024]{1,0:T(8,128)(2,1)} fusion(bf16[512,1024]{1,0:T(8,128)(2,1)S(1)} %copy-done.1, bf16[512,21504]{1,0:T(8,128)(2,1)} %all-gather.8.cloned.1.call-done), kind=kOutput, calls=%fused_computation.3 | convolution fusion | flops 7523532800 | bytes 23068672 | tf_op jit(solution)/shard_map/dot_general | solution.py:20
  470.3 0.0 reduce-scatter.5.cloned.1.call-done
Async XLA Ops:
  7.2 33.1 %all-gather.4.cloned.1.call-start = ((), (), s32[]{:S(2)}) async-start(), calls=%async_computation.2 | async-start | bytes 1310720 | tf_op jit(solution)/shard_map/all_gather | solution.py:33
  7.9 62.5 %all-gather.6.cloned.1.call-start = ((), (), s32[]{:S(2)}) async-start(), calls=%async_computation.3 | async-start | bytes 1310720 | tf_op jit(solution)/shard_map/all_gather | solution.py:34
  8.6 234.8 %reduce-scatter.3.cloned.1.call-start = ((), (), s32[]{:S(2)}) async-start(), calls=%async_computation.4 | async-start | bytes 24772608 | tf_op jit(solution)/shard_map/reduce_scatter | solution.py:40
  40.2 15.1 %copy-start = (bf16[512,1024]{1,0:T(8,128)(2,1)S(1)}, bf16[512,1024]{1,0:T(8,128)(2,1)}, u32[]{:S(2)}) copy-start(bf16[512,1024]{1,0:T(8,128)(2,1)} %all-gather.4.cloned.1.call-done) | copy-start | bytes 3145732
  103.1 257.4 %all-gather.8.cloned.1.call-start = ((), (), s32[]{:S(2)}) async-start(), calls=%async_computation.5 | async-start | bytes 24772608 | tf_op jit(solution)/shard_map/all_gather | solution.py:46
  248.4 221.9 %reduce-scatter.5.cloned.1.call-start = ((), (), s32[]{:S(2)}) async-start(), calls=%async_computation.6 | async-start | bytes 1310720 | tf_op jit(solution)/shard_map/reduce_scatter | solution.py:53
  436.1 20.0 %copy-start.1 = (bf16[512,1024]{1,0:T(8,128)(2,1)S(1)}, bf16[512,1024]{1,0:T(8,128)(2,1)}, u32[]{:S(2)}) copy-start(bf16[512,1024]{1,0:T(8,128)(2,1)} %all-gather.6.cloned.1.call-done) | copy-start | bytes 3145732
Sparse Core Ops, SparseCore 0:
  9.6 30.6 all-gather.3
  41.8 27.4 all-gather.5
  103.3 140.1 reduce-scatter.2
  248.5 112.0 all-gather.7
  387.9 27.1 reduce-scatter.4
where the time goes:
time: 478 us; the launch traced here: 477 us
  waiting for transfers between devices  285 us (60%)
  matrix products  113 us (24%)
  local copies, waits for them, and re-layouts  39.9 us (8%)
  other arithmetic  24.5 us (5%)
  between operations  13.8 us (3%)
    reduce_scatter x1, waiting for transfers between devices, per_device(): lax.psum_scatter(jnp.concatenate([gate_part, up_part, back_part], axis=1)...  140 us
    all_gather x1, waiting for transfers between devices, per_device(): lax.all_gather(activations(sums, columns), 'row', axis=0, tiled=True)  112 us
    dot_general x3, matrix products, contract_rows(): lax.dot_general(left, right, (((0,), (0,)), ((), ())), preferred_element_...  42.6 us
    dot_general x3, matrix products, contract_cols(): lax.dot_general(left, right, (((1,), (1,)), ((), ())), preferred_element_...  40.3 us
    unnamed x6, local copies, waits for them, and re-layouts  39.9 us
    all_gather x1, waiting for transfers between devices, per_device(): lax.all_gather(tokens, 'col', axis=0, tiled=True)  31.5 us
    concatenate x1, other arithmetic, per_device(): jnp.concatenate([gate_part, up_part, back_part], axis=1)  19.6 us
    dot_general x1, matrix products, per_device(): up_part = jnp.dot(x_panel, up_weight, preferred_element_type=jnp.float32)  15.1 us
  transfers between devices with their start and end apart: 5, of which 3 were waited for; matrix products, arithmetic and copies ran while one was open for 24% of the time, Pallas kernels for 0%

commit v1 on v0

--- a/solution.py
+++ b/solution.py
@@ -2,6 +2,19 @@
 import jax.numpy as jnp
 from jax import lax
 from jax.sharding import PartitionSpec as P
+
+
+def gather_around(value, axis, dim):
+    peers, index, span = (lax.axis_size(axis), lax.axis_index(axis), value.shape[dim])
+    forward = [(i, (i + 1) % peers) for i in range(peers)]
+    whole = jnp.zeros((*value.shape[:dim], peers * span, *value.shape[dim + 1 :]), value.dtype)
+    carried = value
+    for lap in range(peers):
+        owner = (index - lap) % peers
+        whole = lax.dynamic_update_slice_in_dim(whole, carried, owner * span, axis=dim)
+        if lap < peers - 1:
+            carried = lax.ppermute(carried, axis, forward)
+    return whole
 
 
 def activations(sums, columns):
@@ -30,7 +43,7 @@
 
 def per_device(tokens, cotangent, gate_weight, up_weight, down_weight):
     x_panel, dy_panel = (
-        lax.all_gather(tokens, "col", axis=0, tiled=True),
+        gather_around(tokens, "col", 0),
         lax.all_gather(cotangent, "col", axis=0, tiled=True),
     )
     columns = gate_weight.shape[1]

time: 478 us -> 433 us (0.906)
  local copies, waits for them, and re-layouts: 39.9 us -> 1.2 us
  matrix products: 113 us -> 108 us
    unnamed x6 -> x10, local copies, waits for them, and re-layouts: 39.9 us -> 0.03 us
    all_gather x1 -> x0, waiting for transfers between devices: 31.5 us -> none  [per_device(): lax.all_gather(tokens, 'col', axis=0, tiled=True)]
    ppermute x0 -> x3, waiting for transfers between devices: none -> 30.8 us  [gather_around(): carried = lax.ppermute(carried, axis, forward)]
    dot_general x1, matrix products: 15 us -> 9.95 us  [per_device(): jnp.dot(x_panel, gate_weight, preferred_element_type=jnp.float32)]
  transfers between devices with their start and end apart: 5 -> 7, of which waited for: 3 -> 5; matrix products, arithmetic and copies ran while one was open for 24% -> 16% of each run, Pallas kernels for 0% -> 0%
where the time goes in v1:
time: 433 us
  waiting for transfers between devices  281 us (65%)
  matrix products  108 us (25%)
  other arithmetic  24.5 us (6%)
  between operations  14 us (3%)
    reduce_scatter x1, waiting for transfers between devices, per_device(): lax.psum_scatter(jnp.concatenate([gate_part, up_part, back_part], axis=1)...  138 us
    all_gather x1, waiting for transfers between devices, per_device(): lax.all_gather(activations(sums, columns), 'row', axis=0, tiled=True)  112 us
    dot_general x3, matrix products, contract_rows(): lax.dot_general(left, right, (((0,), (0,)), ((), ())), preferred_element_...  42.7 us
    dot_general x3, matrix products, contract_cols(): lax.dot_general(left, right, (((1,), (1,)), ((), ())), preferred_element_...  40.4 us
    ppermute x3, waiting for transfers between devices, gather_around(): carried = lax.ppermute(carried, axis, forward)  30.8 us
    concatenate x1, other arithmetic, per_device(): jnp.concatenate([gate_part, up_part, back_part], axis=1)  19.6 us
    dot_general x1, matrix products, per_device(): up_part = jnp.dot(x_panel, up_weight, preferred_element_type=jnp.float32)  15.2 us
    dot_general x1, matrix products, per_device(): jnp.dot(x_panel, gate_weight, preferred_element_type=jnp.float32)  9.95 us
  transfers between devices with their start and end apart: 7, of which 5 were waited for; matrix products, arithmetic and copies ran while one was open for 16% of the time, Pallas kernels for 0%

profile of v1, /device:TPU:0, one launch (start us, length us, event | category | flops | bytes accessed | tf_op | source)
XLA Modules:
  0.0 432.5 jit_solution(14688852444827249374)
XLA Ops:
  7.2 0.0 all-gather.3.cloned.1.call-start
  7.2 3.1 collective-permute-start
  10.3 8.5 %collective-permute-done = bf16[128,1024]{1,0:T(8,128)(2,1)S(1)} collective-permute-done((bf16[128,1024]{1,0:T(8,128)(2,1)}, bf16[128,1024]{1,0:T(8,128)(2,1)S(1)}, u32[]{:S(2)}, u32[]{:S(2)}) %collective-permute-start) | collective-permute-done | bytes 262176 | tf_op jit(solution)/shard_map/ppermute | solution.py:16
  18.8 0.0 collective-permute-start.1
  18.8 0.0 all-gather.3.cloned.1.call-update
  18.9 0.0 reduce-scatter.3.cloned.1.call-start
  18.9 9.2 %collective-permute-done.1 = bf16[128,1024]{1,0:T(8,128)(2,1)S(1)} collective-permute-done((bf16[128,1024]{1,0:T(8,128)(2,1)S(1)}, bf16[128,1024]{1,0:T(8,128)(2,1)S(1)}, u32[]{:S(2)}, u32[]{:S(2)}) %collective-permute-start.1) | collective-permute-done | bytes 262176 | tf_op jit(solution)/shard_map/ppermute | solution.py:16
  28.1 0.0 collective-permute-start.2
  28.1 0.1 broadcast_in_dim.3
  28.2 1.0 constant_dynamic-update-slice_fusion.3
  29.4 13.0 %collective-permute-done.2 = bf16[128,1024]{1,0:T(8,128)(2,1)S(1)} collective-permute-done((bf16[128,1024]{1,0:T(8,128)(2,1)S(1)}, bf16[128,1024]{1,0:T(8,128)(2,1)S(1)}, u32[]{:S(2)}, u32[]{:S(2)}) %collective-permute-start.2) | collective-permute-done | bytes 262176 | tf_op jit(solution)/shard_map/ppermute | solution.py:16
  42.4 0.0 slice-start
  42.4 0.0 slice-start.1
  42.4 0.0 slice-start.2
  42.5 0.0 slice-start.3
  42.5 15.2 %convolution_convert_fusion.4 = bf16[512,7168]{1,0:T(8,128)(2,1)} fusion(bf16[512,1024]{1,0:T(8,128)(2,1)S(1)} %constant_dynamic-update-slice_fusion, bf16[1024,7168]{1,0:T(8,128)(2,1)} %param.8), kind=kOutput, calls=%fused_computation.5 | convolution fusion | flops 7519862784 | bytes 23068672 | tf_op jit(solution)/shard_map/dot_general | solution.py:51
  57.6 0.0 slice-done
  57.7 0.0 slice-done.1
  57.7 0.0 slice-done.2
  57.7 0.0 slice-done.3
  57.7 9.9 %convolution_convert_fusion.5 = bf16[512,7168]{1,0:T(8,128)(2,1)} fusion(bf16[512,1024]{1,0:T(8,128)(2,1)S(1)} %constant_dynamic-update-slice_fusion, bf16[1024,7168]{1,0:T(8,128)(2,1)S(1)} %bitcast.12), kind=kOutput, calls=%fused_computation.6 | convolution fusion | flops 7519862784 | bytes 23068672 | tf_op jit(solution)/shard_map/dot_general | solution.py:50
  67.6 0.0 all-gather.3.cloned.1.call-done
  67.6 13.2 %convolution_convert_fusion.3 = bf16[512,7168]{1,0:T(8,128)(2,1)} fusion(bf16[512,1024]{1,0:T(8,128)(2,1)} %all-gather.3.cloned.1.call-done, bf16[7168,1024]{1,0:T(8,128)(2,1)} %param.9), kind=kOutput, calls=%fused_computation.4 | convolution fusion | flops 7519862784 | bytes 23068672 | tf_op jit(solution)/shard_map/dot_general | solution.py:39
  80.8 19.6 %pad_maximum_fusion = bf16[512,21504]{1,0:T(8,128)(2,1)} fusion(bf16[512,7168]{1,0:T(8,128)(2,1)} %convolution_convert_fusion.3, bf16[512,7168]{1,0:T(8,128)(2,1)} %convolution_convert_fusion.4, bf16[512,7168]{1,0:T(8,128)(2,1)} %convolution_convert_fusion.5), kind=kLoop, calls=%fused_computation | loop fusion | flops 66060288 | bytes 44040192 | tf_op jit(solution)/shard_map/concatenate | solution.py:54
  100.4 0.0 reduce-scatter.3.cloned.1.call-update
  100.4 0.2 all-gather.5.cloned.1.call-start
  100.6 138.2 %reduce-scatter.3.cloned.1.call-done = bf16[64,21504]{1,0:T(8,128)(2,1)} async-done(((bf16[512,21504]{1,0:T(8,128)(2,1)}), bf16[64,21504]{1,0:T(8,128)(2,1)}) %reduce-scatter.3.cloned.1.call-update) | async-done | bytes 2752528 | tf_op jit(solution)/shard_map/reduce_scatter | solution.py:53
  238.9 2.1 convert_element_type.25
  241.0 1.1 multiply_convert_fusion.2
  242.1 1.7 pad_maximum_fusion.1
  243.8 0.0 all-gather.5.cloned.1.call-update
  243.8 0.0 reduce-scatter.5.cloned.1.call-start
  243.9 112.1 %all-gather.5.cloned.1.call-done = bf16[512,21504]{1,0:T(8,128)(2,1)} async-done(((bf16[64,21504]{1,0:T(8,128)(2,1)}), bf16[512,21504]{1,0:T(8,128)(2,1)}) %all-gather.5.cloned.1.call-update) | async-done | bytes 22020112 | tf_op jit(solution)/shard_map/all_gather | solution.py:59
  356.0 13.2 %fusion.2 = f32[512,1024]{1,0:T(8,128)S(1)} fusion(bf16[1024,7168]{1,0:T(8,128)(2,1)} %param.8, bf16[512,21504]{1,0:T(8,128)(2,1)} %all-gather.5.cloned.1.call-done), kind=kOutput, calls=%fused_computation.9 | convolution fusion | flops 7516192768 | bytes 24117248 | tf_op jit(solution)/shard_map/dot_general | solution.py:39
  369.1 14.1 %add_convert_fusion = bf16[512,1024]{1,0:T(8,128)(2,1)} fusion(f32[512,1024]{1,0:T(8,128)S(1)} %fusion.2, bf16[1024,7168]{1,0:T(8,128)(2,1)} %param.7, bf16[512,21504]{1,0:T(8,128)(2,1)} %all-gather.5.cloned.1.call-done), kind=kOutput, calls=%fused_computation.15 | convolution fusion | flops 7517241344 | bytes 25165824 | tf_op jit(solution)/shard_map/dot_general | solution.py:39
  383.2 0.0 reduce-scatter.5.cloned.1.call-update
  383.3 0.0 copy-start
  383.3 14.3 %convolution_convert_fusion.2 = bf16[1024,7168]{1,0:T(8,128)(2,1)} fusion(bf16[512,1024]{1,0:T(8,128)(2,1)S(1)} %constant_dynamic-update-slice_fusion, bf16[512,21504]{1,0:T(8,128)(2,1)} %all-gather.5.cloned.1.call-done), kind=kOutput, calls=%fused_computation.3 | convolution fusion | flops 7523532800 | bytes 23068672 | tf_op jit(solution)/shard_map/dot_general | solution.py:33
  397.6 0.0 copy-done
  397.6 14.2 %convolution_convert_fusion = bf16[7168,1024]{1,0:T(8,128)(2,1)} fusion(bf16[512,1024]{1,0:T(8,128)(2,1)S(1)} %copy-done, bf16[512,21504]{1,0:T(8,128)(2,1)} %all-gather.5.cloned.1.call-done), kind=kOutput, calls=%fused_computation.1 | convolution fusion | flops 7523532800 | bytes 23068672 | tf_op jit(solution)/shard_map/dot_general | solution.py:33
  411.8 14.2 %convolution_convert_fusion.1 = bf16[1024,7168]{1,0:T(8,128)(2,1)} fusion(bf16[512,1024]{1,0:T(8,128)(2,1)S(1)} %constant_dynamic-update-slice_fusion, bf16[512,21504]{1,0:T(8,128)(2,1)} %all-gather.5.cloned.1.call-done), kind=kOutput, calls=%fused_computation.2 | convolution fusion | flops 7523532800 | bytes 23068672 | tf_op jit(solution)/shard_map/dot_general | solution.py:33
  426.0 0.0 reduce-scatter.5.cloned.1.call-done
  (4 shorter events, 0.1 us)
Async XLA Ops:
  7.2 60.5 %all-gather.3.cloned.1.call-start = ((), (), s32[]{:S(2)}) async-start(), calls=%async_computation.2 | async-start | bytes 1310720 | tf_op jit(solution)/shard_map/all_gather | solution.py:47
  7.2 11.6 %collective-permute-start = (bf16[128,1024]{1,0:T(8,128)(2,1)}, bf16[128,1024]{1,0:T(8,128)(2,1)S(1)}, u32[]{:S(2)}, u32[]{:S(2)}) collective-permute-start(bf16[128,1024]{1,0:T(8,128)(2,1)} %param.5), channel_id=1, source_target_pairs={{0,1},{1,2},{2,3},{3,0},{4,5},{5,6},{6,7},{7,4},{8,9},{9,10},{10,1... | collective-permute-start | bytes 786440 | tf_op jit(solution)/shard_map/ppermute | solution.py:16
  18.8 9.3 %collective-permute-start.1 = (bf16[128,1024]{1,0:T(8,128)(2,1)S(1)}, bf16[128,1024]{1,0:T(8,128)(2,1)S(1)}, u32[]{:S(2)}, u32[]{:S(2)}) collective-permute-start(bf16[128,1024]{1,0:T(8,128)(2,1)S(1)} %collective-permute-done), channel_id=1, source_target_pairs={{0,1},{1,2},{2,3},{3,0},{4,5},{5,6},{6,7},{7,4},{8,9},{9,10},{10,1... | collective-permute-start | bytes 786440 | tf_op jit(solution)/shard_map/ppermute | solution.py:16
  18.9 220.0 %reduce-scatter.3.cloned.1.call-start = ((), (), s32[]{:S(2)}) async-start(), calls=%async_computation.3 | async-start | bytes 24772608 | tf_op jit(solution)/shard_map/reduce_scatter | solution.py:53
  28.1 14.3 %collective-permute-start.2 = (bf16[128,1024]{1,0:T(8,128)(2,1)S(1)}, bf16[128,1024]{1,0:T(8,128)(2,1)S(1)}, u32[]{:S(2)}, u32[]{:S(2)}) collective-permute-start(bf16[128,1024]{1,0:T(8,128)(2,1)S(1)} %collective-permute-done.1), channel_id=1, source_target_pairs={{0,1},{1,2},{2,3},{3,0},{4,5},{5,6},{6,7},{7,4},{8,9},{9,10},{10,1... | collective-permute-start | bytes 786440 | tf_op jit(solution)/shard_map/ppermute | solution.py:16
  42.4 15.2 %slice-start = ((s8[14680064]{0:T(1024)(128)(4,1)}), s8[4194304]{0:T(1024)(128)(4,1)S(1)}, s32[]{:S(2)}) async-start(s8[14680064]{0:T(1024)(128)(4,1)} %bitcast.11), calls=%async_computation.6 | async-start | bytes 8388608
  42.4 15.2 %slice-start.1 = ((s8[14680064]{0:T(1024)(128)(4,1)}), s8[4194304]{0:T(1024)(128)(4,1)S(1)}, s32[]{:S(2)}) async-start(s8[14680064]{0:T(1024)(128)(4,1)} %bitcast.11), calls=%async_computation.7 | async-start | bytes 8388608
  42.4 15.2 %slice-start.2 = ((s8[14680064]{0:T(1024)(128)(4,1)}), s8[4194304]{0:T(1024)(128)(4,1)S(1)}, s32[]{:S(2)}) async-start(s8[14680064]{0:T(1024)(128)(4,1)} %bitcast.11), calls=%async_computation.8 | async-start | bytes 8388608
  42.5 15.2 %slice-start.3 = ((s8[14680064]{0:T(1024)(128)(4,1)}), s8[2097152]{0:T(1024)(128)(4,1)S(1)}, s32[]{:S(2)}) async-start(s8[14680064]{0:T(1024)(128)(4,1)} %bitcast.11), calls=%async_computation.9 | async-start | bytes 4194304
  100.4 255.6 %all-gather.5.cloned.1.call-start = ((), (), s32[]{:S(2)}) async-start(), calls=%async_computation.4 | async-start | bytes 24772608 | tf_op jit(solution)/shard_map/all_gather | solution.py:59
  243.8 182.2 %reduce-scatter.5.cloned.1.call-start = ((), (), s32[]{:S(2)}) async-start(), calls=%async_computation.5 | async-start | bytes 1310720 | tf_op jit(solution)/shard_map/reduce_scatter | solution.py:66
  383.3 14.3 %copy-start = (bf16[512,1024]{1,0:T(8,128)(2,1)S(1)}, bf16[512,1024]{1,0:T(8,128)(2,1)}, u32[]{:S(2)}) copy-start(bf16[512,1024]{1,0:T(8,128)(2,1)} %all-gather.3.cloned.1.call-done) | copy-start | bytes 3145732
Sparse Core Ops, SparseCore 0:
  19.0 34.7 all-gather.2
  100.5 138.2 reduce-scatter.2
  243.9 111.9 all-gather.4
  383.4 27.1 reduce-scatter.4
